TPU v7x, 512 devices: a whole 4x8x8 slice. The times are simulated.
512 devices in a mesh: seq: 32 (over x, y), head: 8 (over z), doc: 2 (over core).
Axes of the slice: x: 4, y: 8, z: 8, core: 2. Of those that a mesh axis runs over, the one named last changes fastest.
Arguments:
- byte_states: bfloat16 [32768, 1024], P(('doc', 'seq')), parts along dimension 0, may hold values from -36 to 36
- conv_kernel: float32 [4, 1024], replicated, may hold values from -3 to 3
- mix_weight: bfloat16 [1024, 1024], replicated, may hold values from -0.1875 to 0.1875
- norm_gain: float32 [1024], replicated, may hold values from 0.1 to 1.9
- query_weight: bfloat16 [1024, 1024], P(None, 'head'), may hold values from -3 to 3
- key_weight: bfloat16 [1024, 1024], P(None, 'head'), may hold values from -3 to 3
- value_weight: bfloat16 [1024, 1024], P(None, 'head'), may hold values from -0.1875 to 0.1875
- boundaries: int32 [4096], P(('doc', 'seq')), parts along dimension 0, may hold values from 0 to 511, as said below
- span_counts: int32 [64], P(('doc', 'seq')), parts along dimension 0, may hold values from 16 to 64, as said below
- grad_attended: bfloat16 [4096, 1024], P(('doc', 'seq'), 'head'), parts along dimension 0, may hold values from -6 to 6
Outputs:
- attended: bfloat16 [4096, 1024], P(('doc', 'seq'), 'head'), parts along dimension 0
- grad_bytes: bfloat16 [32768, 1024], P(('doc', 'seq')), parts along dimension 0
There are 2 independent parts, one for each index of `doc`. A program takes and returns all parts, laid end to end along the dimension named above; an argument that names none is the same for every part. Nothing has to cross between parts.
Inputs may be any that keep to these rules, and one draw needn't show every extreme that they name: `span_counts`: number of spans starting in each shard; in every draw some shard has exactly 64. `boundaries`: in each shard's 64 slots the first span_counts entries are strictly increasing byte positions inside the shard, the first of them 0; the remaining slots hold 0.
All inputs are finite; a program needn't handle non-finite values.
Results may differ from a plain program's by a relative error of at most 0.017.
Values may be sent and summed in bfloat16 or wider, within the bound.
No kernel may reach another device: no remote copies, remote signals or barrier semaphores. Data moves between devices by JAX's collectives and lax.ppermute only.
A program may use at most 64 MiB of HBM per device.

v0:
```python
import math
import jax
import jax.numpy as jnp
from jax import lax
from jax.sharding import PartitionSpec as P

D = 1024
HD = 128
KCONV = 4
masked_score = -1e30


def passed_along(array, axis, by):
    devices = lax.axis_size(axis)
    pairs = [(i, i + by) for i in range(devices) if 0 <= i + by < devices]
    return lax.ppermute(array, axis, pairs)


def neighbour(rim_rows, offset_by):
    return passed_along(rim_rows, "seq", offset_by)


def per_device(
    byte_states,
    conv_kernel,
    mix_weight,
    norm_gain,
    query_weight,
    key_weight,
    value_weight,
    boundaries,
    span_counts,
    grad_attended,
):
    row_count = byte_states.shape[0]
    slot_count = boundaries.shape[0]
    head_width = query_weight.shape[1]
    local_heads = head_width // HD
    score_scale = 1.0 / math.sqrt(HD)
    shard_index = lax.axis_index("seq")
    first_slot = shard_index * slot_count
    own_ids = first_slot + jnp.arange(slot_count, dtype=jnp.int32)
    before_rim = neighbour(byte_states[row_count - (KCONV - 1) :].astype(jnp.float32), 1)
    extended = jnp.concatenate([before_rim.astype(jnp.bfloat16), byte_states], axis=0)
    span_depth = conv_kernel[0] * jnp.take(extended, boundaries + (KCONV - 1), axis=0).astype(
        jnp.float32
    )
    for offset in range(1, KCONV):
        tapped = jnp.take(extended, boundaries + (KCONV - 1 - offset), axis=0).astype(jnp.float32)
        span_depth = span_depth + conv_kernel[offset] * tapped
    span_depth = span_depth.astype(jnp.bfloat16)
    span_bytes = jnp.take(byte_states, boundaries, axis=0).astype(jnp.float32)
    live_mask = jnp.arange(slot_count, dtype=jnp.int32) < span_counts[0]
    live_half = live_mask.astype(jnp.bfloat16)
    span_state = span_bytes + jnp.dot(span_depth, mix_weight, preferred_element_type=jnp.float32)
    inverse_rms = lax.rsqrt(jnp.mean(span_state * span_state, axis=1) + 1e-05)
    normed = (span_state * inverse_rms[:, None] * norm_gain).astype(jnp.bfloat16)
    queries = jnp.dot(normed, query_weight, preferred_element_type=jnp.float32).astype(jnp.bfloat16)
    key_rows = jnp.dot(normed, key_weight, preferred_element_type=jnp.float32).astype(jnp.bfloat16)
    value_rows = jnp.dot(normed, value_weight, preferred_element_type=jnp.float32).astype(
        jnp.bfloat16
    )
    grad_rows = jnp.where(live_mask[:, None], grad_attended, jnp.zeros_like(grad_attended))
    query_heads = queries.reshape(slot_count, local_heads, HD)
    key_heads = key_rows.reshape(slot_count, local_heads, HD)
    value_heads = value_rows.reshape(slot_count, local_heads, HD)
    grad_heads = grad_rows.reshape(slot_count, local_heads, HD)
    piece_keys = lax.all_gather(key_rows, "seq", axis=0, tiled=True)
    piece_values = lax.all_gather(value_rows, "seq", axis=0, tiled=True)
    piece_live = lax.all_gather(live_half, "seq", axis=0, tiled=True)
    running_max = jnp.full((local_heads, slot_count), masked_score, jnp.float32)
    piece_rows = piece_keys.shape[0]
    key_ids = jnp.arange(piece_rows, dtype=jnp.int32)
    allowed = (key_ids[None, :] <= own_ids[:, None]) & (piece_live[None, :] > 0.5)
    scores = (
        jnp.einsum(
            "qhd,khd->hqk",
            query_heads,
            piece_keys.reshape(piece_rows, local_heads, HD),
            preferred_element_type=jnp.float32,
        )
        * score_scale
    )
    scores = jnp.where(allowed[None], scores, masked_score)
    new_max = jnp.maximum(running_max, jnp.max(scores, axis=2))
    softmax_part = jnp.exp(scores - new_max[:, :, None])
    new_sum = jnp.sum(softmax_part, axis=2)
    product = jnp.einsum(
        "hqk,khd->hqd",
        softmax_part.astype(jnp.bfloat16),
        piece_values.reshape(piece_rows, local_heads, HD),
        preferred_element_type=jnp.float32,
    )
    attention = jnp.transpose(product / new_sum[:, :, None], (1, 0, 2)).reshape(
        slot_count, head_width
    )
    attended = jnp.where(live_mask[:, None], attention, jnp.float32(0.0)).astype(jnp.bfloat16)
    log_rows = jnp.transpose(new_max + jnp.log(new_sum))
    delta_rows = jnp.sum(
        grad_heads.astype(jnp.float32)
        * attended.reshape(slot_count, local_heads, HD).astype(jnp.float32),
        axis=2,
    )
    own_logs = jnp.transpose(log_rows)
    own_deltas = jnp.transpose(delta_rows)
    all_logs, all_deltas = (
        lax.all_gather(log_rows, "seq", axis=0, tiled=True),
        lax.all_gather(delta_rows, "seq", axis=0, tiled=True),
    )
    piece_queries = lax.all_gather(queries, "seq", axis=0, tiled=True)
    piece_keys = lax.all_gather(key_rows, "seq", axis=0, tiled=True)
    piece_values = lax.all_gather(value_rows, "seq", axis=0, tiled=True)
    piece_grads = lax.all_gather(grad_rows, "seq", axis=0, tiled=True)
    piece_live = lax.all_gather(live_half, "seq", axis=0, tiled=True)
    piece_rows = piece_keys.shape[0]
    key_ids = jnp.arange(piece_rows, dtype=jnp.int32)
    key_part = piece_keys.reshape(piece_rows, local_heads, HD)
    allowed = (key_ids[None, :] <= own_ids[:, None]) & (piece_live[None, :] > 0.5)
    scores = (
        jnp.einsum("qhd,khd->hqk", query_heads, key_part, preferred_element_type=jnp.float32)
        * score_scale
    )
    scores = jnp.where(allowed[None], scores, masked_score)
    probs_full = jnp.exp(scores - own_logs[:, :, None])
    grad_probs = jnp.einsum(
        "qhd,khd->hqk",
        grad_heads,
        piece_values.reshape(piece_rows, local_heads, HD),
        preferred_element_type=jnp.float32,
    )
    grad_scores = (probs_full * (grad_probs - own_deltas[:, :, None])).astype(jnp.bfloat16)
    new_query = jnp.einsum(
        "hqk,khd->hqd", grad_scores, key_part, preferred_element_type=jnp.float32
    )
    piece_rows = piece_queries.shape[0]
    piece_ids = jnp.arange(piece_rows, dtype=jnp.int32)
    query_part = piece_queries.reshape(piece_rows, local_heads, HD)
    grad_part = piece_grads.reshape(piece_rows, local_heads, HD)
    piece_logs = jnp.transpose(all_logs)
    piece_deltas = jnp.transpose(all_deltas)
    allowed = (own_ids[None, :] <= piece_ids[:, None]) & live_mask[None, :]
    scores = (
        jnp.einsum("qhd,khd->hqk", query_part, key_heads, preferred_element_type=jnp.float32)
        * score_scale
    )
    scores = jnp.where(allowed[None], scores, masked_score)
    probs_full = jnp.exp(scores - piece_logs[:, :, None])
    grad_value = jnp.einsum(
        "hqk,qhd->hkd",
        probs_full.astype(jnp.bfloat16),
        grad_part,
        preferred_element_type=jnp.float32,
    )
    grad_probs = jnp.einsum(
        "qhd,khd->hqk", grad_part, value_heads, preferred_element_type=jnp.float32
    )
    grad_scores = (probs_full * (grad_probs - piece_deltas[:, :, None])).astype(jnp.bfloat16)
    grad_key = jnp.einsum(
        "hqk,qhd->hkd", grad_scores, query_part, preferred_element_type=jnp.float32
    )

    def to_rows(stacked):
        return jnp.transpose(stacked, (1, 0, 2)).reshape(slot_count, head_width)

    contract = (((1,), (1,)), ((), ()))
    query_grad_rows = (to_rows(new_query) * score_scale).astype(jnp.bfloat16)
    key_grad_rows = (to_rows(grad_key) * score_scale).astype(jnp.bfloat16)
    value_grad_rows = to_rows(grad_value).astype(jnp.bfloat16)
    partial_normed = lax.dot_general(
        query_grad_rows, query_weight, contract, preferred_element_type=jnp.float32
    )
    partial_normed = partial_normed + lax.dot_general(
        key_grad_rows, key_weight, contract, preferred_element_type=jnp.float32
    )
    partial_normed = partial_normed + lax.dot_general(
        value_grad_rows, value_weight, contract, preferred_element_type=jnp.float32
    )
    grad_normed = lax.psum(partial_normed.astype(jnp.bfloat16), "head").astype(jnp.float32)
    scaled_grad = norm_gain * grad_normed
    cubed = inverse_rms * inverse_rms * inverse_rms
    grad_state = (
        inverse_rms[:, None] * scaled_grad
        - span_state * cubed[:, None] * jnp.mean(scaled_grad * span_state, axis=1)[:, None]
    )
    grad_state = jnp.where(live_mask[:, None], grad_state, jnp.float32(0.0))
    mixed_grad = lax.dot_general(
        grad_state.astype(jnp.bfloat16), mix_weight, contract, preferred_element_type=jnp.float32
    )
    spread_mix = jnp.zeros((row_count, D), jnp.float32).at[boundaries].add(mixed_grad)
    residual_grad = jnp.zeros((row_count, D), jnp.float32).at[boundaries].add(grad_state)
    after_rim = neighbour(spread_mix[: KCONV - 1], -1)
    padded_grad = jnp.concatenate([spread_mix, after_rim], axis=0)
    conv_grad = conv_kernel[0] * spread_mix
    for offset in range(1, KCONV):
        conv_grad = conv_grad + conv_kernel[offset] * padded_grad[offset : offset + row_count]
    grad_bytes = (residual_grad + conv_grad).astype(jnp.bfloat16)
    return (attended, grad_bytes)


def solution(mesh):
    return jax.shard_map(
        per_device,
        mesh=mesh,
        in_specs=(
            P(("doc", "seq"), None),
            P(),
            P(),
            P(),
            P(None, "head"),
            P(None, "head"),
            P(None, "head"),
            P(("doc", "seq")),
            P(("doc", "seq")),
            P(("doc", "seq"), "head"),
        ),
        out_specs=(P(("doc", "seq"), "head"), P(("doc", "seq"), None)),
        check_vma=False,
    )
```

profile of v0, /device:TPU:56, one launch (start us, length us, event | category | flops | bytes accessed | tf_op | source)
XLA Modules:
  0.0 557.7 jit_solution(17123047837741712854)
XLA Ops:
  7.2 0.0 copy-start
  7.2 0.0 all-reduce.6.cloned.1.call-start
  7.2 0.9 slice.68
  8.1 2.6 collective-permute-start
  10.7 0.7 compare_select_fusion.1
  11.4 1.3 compare_and_fusion.4
  13.3 0.5 iota_add_fusion
  13.8 1.3 dynamic-slice
  15.8 0.2 dynamic-update-slice
  16.0 63.5 %all-reduce = bf16[2048]{0:T(1024)(128)(2,1)S(1)} all-reduce(bf16[2048]{0:T(1024)(128)(2,1)S(1)} %dynamic-update-slice), channel_id=1, replica_groups=mesh['seq'=32,'head'=8,'doc'=2] {'seq'}, use_global_device_ids=true, to_apply=%add | all-reduce | flops 2048 | bytes 8192
  79.5 0.6 broadcast_compare_fusion
  80.1 1.5 fusion.54
  81.6 0.0 copy-done.15
  81.6 0.5 iota_compare_fusion.2
  82.1 2.2 gather_fusion
  84.3 0.0 collective-permute-done
  84.3 1.5 pad_maximum_fusion
  85.8 1.4 gather_fusion.4
  87.2 1.4 gather_fusion.3
  88.5 1.3 gather_fusion.2
  89.9 1.4 gather_fusion.1
  91.2 0.0 copy-done
  91.2 1.9 multiply_reduce_fusion.1
  93.2 0.0 copy-start.12
  93.2 0.0 copy-start.14
  93.2 0.0 copy-done.9
  93.2 0.1 multiply_convert_fusion
  93.3 0.0 copy-done.8
  93.3 0.2 convolution_convert_fusion.1
  93.5 0.0 copy-done.6
  93.5 0.0 copy-start.11
  93.5 0.0 copy-start.13
  93.5 0.2 convolution_convert_fusion.2
  93.7 0.2 convolution_convert_fusion.3
  93.9 60.8 %all_gather.27 = bf16[2048,128]{1,0:T(8,128)(2,1)} all-gather(bf16[64,128]{1,0:T(8,128)(2,1)S(1)} %convolution_convert_fusion.3), channel_id=1, replica_groups=mesh['seq'=32,'head'=8,'doc'=2] {'seq'}, dimensions={0}, use_global_device_ids=true | all-gather | bytes 540672 | tf_op jit(solution)/shard_map/all_gather | solution.py:110
  154.7 48.0 %all_gather.25 = bf16[2048,128]{1,0:T(8,128)(2,1)S(1)} all-gather(bf16[64,128]{1,0:T(8,128)(2,1)S(1)} %convolution_convert_fusion.2), channel_id=1, replica_groups=mesh['seq'=32,'head'=8,'doc'=2] {'seq'}, dimensions={0}, use_global_device_ids=true | all-gather | bytes 540672 | tf_op jit(solution)/shard_map/all_gather | solution.py:68
  202.7 0.0 copy-start.2
  202.7 0.4 fusion.55
  203.1 47.6 %all_gather.26 = bf16[2048,128]{1,0:T(8,128)(2,1)S(1)} all-gather(bf16[64,128]{1,0:T(8,128)(2,1)S(1)} %convolution_convert_fusion.1), channel_id=1, replica_groups=mesh['seq'=32,'head'=8,'doc'=2] {'seq'}, dimensions={0}, use_global_device_ids=true | all-gather | bytes 540672 | tf_op jit(solution)/shard_map/all_gather | solution.py:69
  250.8 0.2 fusion.26
  251.0 0.1 fusion.53
  251.1 1.0 multiply_reduce_fusion.2
  252.2 48.0 %all_gather.29 = bf16[2048,128]{1,0:T(8,128)(2,1)S(1)} all-gather(bf16[64,128]{1,0:T(8,128)(2,1)S(1)} %get-tuple-element.8), channel_id=1, replica_groups=mesh['seq'=32,'head'=8,'doc'=2] {'seq'}, dimensions={0}, use_global_device_ids=true | all-gather | bytes 540672 | tf_op jit(solution)/shard_map/all_gather | solution.py:113
  300.2 1.7 fusion.19
  301.8 0.0 copy-start.4
  301.8 0.3 dynamic-update-slice.2
  302.1 1.8 fusion.56
  304.0 126.1 %all-reduce.3 = (f32[2048]{0:T(1024)S(1)}, f32[2048]{0:T(1024)S(1)}) all-reduce(f32[2048]{0:T(1024)S(1)} %get-tuple-element.5, f32[2048]{0:T(1024)S(1)} %dynamic-update-slice.2), channel_id=2, replica_groups=mesh['seq'=32,'head'=8,'doc'=2] {'seq'}, use_global_device_ids=true, to_apply=%add.1 | all-reduce | flops 4096 | bytes 32768
  430.1 2.2 fusion.5
  432.3 1.5 fusion.18
  433.7 1.2 convolution_add_fusion.1
  435.0 2.1 fusion.13
  437.1 0.0 all-reduce.6.cloned.1.call-update
  437.2 90.4 %all-reduce.6.cloned.1.call-done = bf16[64,1024]{1,0:T(8,128)(2,1)} async-done(((bf16[64,1024]{1,0:T(8,128)(2,1)}), bf16[64,1024]{1,0:T(8,128)(2,1)}) %all-reduce.6.cloned.1.call-update) | async-done | bytes 131088 | tf_op jit(solution)/shard_map/psum | solution.py:178
  527.6 1.0 multiply_reduce_fusion
  528.7 1.7 fusion.39
  530.3 2.6 scatter_custom_fusion
  533.0 0.8 slice.50
  533.7 3.5 collective-permute-start.1
  537.2 1.8 constant_dynamic-update-slice_fusion.1
  539.1 2.5 collective-permute-done.1
  541.6 2.2 fusion.8
  543.9 4.2 scatter_custom_fusion.1
  548.1 2.7 convert_element_type.113
  (31 shorter events, 0.1 us)
Async XLA Ops:
  7.2 84.1 %copy-start = (bf16[1024,1024]{1,0:T(8,128)(2,1)S(1)}, bf16[1024,1024]{1,0:T(8,128)(2,1)}, u32[]{:S(2)}) copy-start(bf16[1024,1024]{1,0:T(8,128)(2,1)} %param.14) | copy-start | bytes 6291460
  7.2 520.4 %all-reduce.6.cloned.1.call-start = ((), (), s32[]{:S(2)}) async-start(), calls=%async_computation | async-start | bytes 262144 | tf_op jit(solution)/shard_map/psum | solution.py:178
  8.1 76.2 %collective-permute-start = (bf16[3,1024]{1,0:T(4,128)(2,1)S(1)}, bf16[3,1024]{1,0:T(4,128)(2,1)S(1)}, u32[]{:S(2)}, u32[]{:S(2)}) collective-permute-start(bf16[3,1024]{1,0:T(4,128)(2,1)S(1)} %slice.68), channel_id=1, source_target_pairs={{0,16},{16,32},{32,48},{48,64},{64,80},{80,96},{96,112},{112,128},... | collective-permute-start | bytes 18440 | tf_op jit(solution)/shard_map/ppermute | solution.py:16
  11.4 70.2 %copy-start.15 = (s32[64]{0:T(128)}, s32[64]{0:T(128)S(1)}, u32[]{:S(2)}) copy-start(s32[64]{0:T(128)S(1)} %get-tuple-element.29) | copy-start | bytes 772
  89.9 3.4 copy-start.9
  91.2 2.1 copy-start.8
  91.2 2.3 copy-start.6
  91.2 2.5 copy-start.7
  93.2 109.5 %copy-start.12 = (pred[2048]{0:T(1024)(128)(4,1)S(1)}, pred[2048]{0:T(1024)(128)(4,1)}, u32[]{:S(2)}) copy-start(pred[2048]{0:T(1024)(128)(4,1)} %broadcast_compare_fusion) | copy-start | bytes 6148
  93.2 109.5 %copy-start.14 = (s32[64]{0:T(128)S(1)}, s32[64]{0:T(128)}, u32[]{:S(2)}) copy-start(s32[64]{0:T(128)} %iota_add_fusion) | copy-start | bytes 772
  93.5 157.6 %copy-start.11 = (bf16[64,128]{1,0:T(8,128)(2,1)S(1)}, bf16[64,128]{1,0:T(8,128)(2,1)}, u32[]{:S(2)}) copy-start(bf16[64,128]{1,0:T(8,128)(2,1)} %param.21) | copy-start | bytes 49156
  93.5 157.6 %copy-start.13 = (pred[64]{0:T(512)(128)(4,1)S(1)}, pred[64]{0:T(512)(128)(4,1)}, u32[]{:S(2)}) copy-start(pred[64]{0:T(512)(128)(4,1)} %iota_compare_fusion.2) | copy-start | bytes 196
  202.7 49.4 %copy-start.2 = (bf16[2048,128]{1,0:T(8,128)(2,1)}, bf16[2048,128]{1,0:T(8,128)(2,1)S(1)}, u32[]{:S(2)}) copy-start(bf16[2048,128]{1,0:T(8,128)(2,1)S(1)} %all_gather.25) | copy-start | bytes 1572868
  250.7 1.4 copy-start.3
  301.8 130.4 %copy-start.4 = (bf16[2048,128]{1,0:T(8,128)(2,1)S(1)}, bf16[2048,128]{1,0:T(8,128)(2,1)}, u32[]{:S(2)}) copy-start(bf16[2048,128]{1,0:T(8,128)(2,1)} %all_gather.27) | copy-start | bytes 1572868
  533.7 7.9 %copy-start.1 = (f32[512,1024]{1,0:T(8,128)S(1)}, f32[512,1024]{1,0:T(8,128)}, u32[]{:S(2)}) copy-start(f32[512,1024]{1,0:T(8,128)} %scatter_custom_fusion) | copy-start | bytes 6291460
  533.7 7.9 %copy-start.10 = (f32[1,1024]{1,0:T(1,128)S(1)}, f32[1,1024]{1,0:T(1,128)}, u32[]{:S(2)}) copy-start(f32[1,1024]{1,0:T(1,128)} %get-tuple-element.18) | copy-start | bytes 12292
  533.7 7.9 %collective-permute-start.1 = (f32[3,1024]{1,0:T(4,128)S(1)}, f32[3,1024]{1,0:T(4,128)S(1)}, u32[]{:S(2)}, u32[]{:S(2)}) collective-permute-start(f32[3,1024]{1,0:T(4,128)S(1)} %slice.50), channel_id=1, source_target_pairs={{16,0},{32,16},{48,32},{64,48},{80,64},{96,80},{112,96},{128,112},... | collective-permute-start | bytes 36872 | tf_op jit(solution)/shard_map/ppermute | solution.py:16
  541.6 2.2 copy-start.5
Sparse Core Ops, SparseCore 0:
  437.3 90.2 all-reduce.5
where the time goes:
time: 559 us; the launch traced here: 558 us
  blocking collectives  394 us (70%)
  waiting for transfers between devices  93 us (17%)
  other arithmetic  18.4 us (3%)
  matrix products  16.1 us (3%)
  between operations  15.6 us (3%)
  local copies, waits for them, and re-layouts  14.4 us (3%)
  starting transfers between devices  6.1 us (1%)
    unnamed x2, blocking collectives  190 us
    psum x1, waiting for transfers between devices, per_device(): lax.psum(partial_normed.astype(jnp.bfloat16), 'head').astype(jnp.float32)  90.4 us
    all_gather x1, blocking collectives, per_device(): piece_queries = lax.all_gather(queries, 'seq', axis=0, tiled=True)  60.8 us
    all_gather x1, blocking collectives, per_device(): piece_grads = lax.all_gather(grad_rows, 'seq', axis=0, tiled=True)  48 us
    all_gather x1, blocking collectives, per_device(): piece_keys = lax.all_gather(key_rows, 'seq', axis=0, tiled=True)  48 us
    all_gather x1, blocking collectives, per_device(): piece_values = lax.all_gather(value_rows, 'seq', axis=0, tiled=True)  47.6 us
  transfers between devices with their start and end apart: 3, of which 2 were waited for; matrix products, arithmetic and copies ran while one was open for 2% of the time, Pallas kernels for 0%

commit v1 on v0

--- a/solution.py
+++ b/solution.py
@@ -32,6 +32,13 @@
     span_counts,
     grad_attended,
 ):
+
+    def edges_extend(mine, across):
+        z1 = jnp.stack([mine for _ in range(lax.axis_size(across))])
+        ready = lax.all_to_all(z1, axis_name=across, split_axis=0, concat_axis=0)
+        v_next = jnp.concatenate(ready, 0)
+        return v_next
+
     row_count = byte_states.shape[0]
     slot_count = boundaries.shape[0]
     head_width = query_weight.shape[1]
@@ -110,7 +117,7 @@
     piece_queries = lax.all_gather(queries, "seq", axis=0, tiled=True)
     piece_keys = lax.all_gather(key_rows, "seq", axis=0, tiled=True)
     piece_values = lax.all_gather(value_rows, "seq", axis=0, tiled=True)
-    piece_grads = lax.all_gather(grad_rows, "seq", axis=0, tiled=True)
+    piece_grads = edges_extend(grad_rows, "seq")
     piece_live = lax.all_gather(live_half, "seq", axis=0, tiled=True)
     piece_rows = piece_keys.shape[0]
     key_ids = jnp.arange(piece_rows, dtype=jnp.int32)

time: 559 us -> 523 us (0.936)
  blocking collectives: 394 us -> 362 us
  waiting for transfers between devices: 93 us -> 80.4 us
  starting transfers between devices: 6.1 us -> 12.8 us
    all_gather x1 -> x0, blocking collectives: 48 us -> none  [per_device(): piece_grads = lax.all_gather(grad_rows, 'seq', axis=0, tiled=True)]
    psum x1, waiting for transfers between devices: 90.4 us -> 77.8 us  [per_device(): lax.psum(partial_normed.astype(jnp.bfloat16), 'head').astype(jnp.float32)]
    all_gather x1, blocking collectives: 48 us -> 56.4 us  [per_device(): piece_keys = lax.all_gather(key_rows, 'seq', axis=0, tiled=True)]
    all_to_all x0 -> x1, starting transfers between devices: none -> 6.66 us  [edges_extend(): ready = lax.all_to_all(z1, axis_name=across, split_axis=0, concat_axis=0)]
  transfers between devices with their start and end apart: 3 -> 4, of which waited for: 2 -> 2; matrix products, arithmetic and copies ran while one was open for 2% -> 3% of each run, Pallas kernels for 0% -> 0%
where the time goes in v1:
time: 523 us; the launch traced here: 522 us
  blocking collectives  362 us (69%)
  waiting for transfers between devices  80.4 us (15%)
  other arithmetic  18.4 us (4%)
  local copies, waits for them, and re-layouts  16.6 us (3%)
  matrix products  16.1 us (3%)
  between operations  15.6 us (3%)
  starting transfers between devices  12.8 us (2%)
    unnamed x2, blocking collectives  191 us
    psum x1, waiting for transfers between devices, per_device(): lax.psum(partial_normed.astype(jnp.bfloat16), 'head').astype(jnp.float32)  77.8 us
    all_gather x1, blocking collectives, per_device(): piece_queries = lax.all_gather(queries, 'seq', axis=0, tiled=True)  66.1 us
    all_gather x1, blocking collectives, per_device(): piece_keys = lax.all_gather(key_rows, 'seq', axis=0, tiled=True)  56.4 us
    all_gather x1, blocking collectives, per_device(): piece_values = lax.all_gather(value_rows, 'seq', axis=0, tiled=True)  48.4 us
  transfers between devices with their start and end apart: 4, of which 2 were waited for; matrix products, arithmetic and copies ran while one was open for 3% of the time, Pallas kernels for 0%

profile of v1, /device:TPU:56, one launch (start us, length us, event | category | flops | bytes accessed | tf_op | source)
XLA Modules:
  0.0 522.0 jit_solution(2005950302565231299)
XLA Ops:
  7.2 0.0 copy-start
  7.2 0.9 slice.68
  8.1 2.6 collective-permute-start
  10.7 0.7 compare_select_fusion.1
  11.3 1.2 compare_and_fusion.4
  13.2 0.5 iota_add_fusion
  13.7 1.3 dynamic-slice
  15.7 0.2 dynamic-update-slice
  15.9 63.5 %all-reduce = bf16[2048]{0:T(1024)(128)(2,1)S(1)} all-reduce(bf16[2048]{0:T(1024)(128)(2,1)S(1)} %dynamic-update-slice), channel_id=1, replica_groups=mesh['seq'=32,'head'=8,'doc'=2] {'seq'}, use_global_device_ids=true, to_apply=%add | all-reduce | flops 2048 | bytes 8192
  79.5 0.6 broadcast_compare_fusion
  80.0 1.5 fusion.54
  81.5 0.0 copy-done.16
  81.5 0.5 iota_compare_fusion.2
  82.1 2.2 gather_fusion
  84.2 0.0 collective-permute-done
  84.3 1.5 pad_maximum_fusion
  85.8 1.4 gather_fusion.4
  87.1 1.3 gather_fusion.3
  88.5 1.4 gather_fusion.2
  89.8 1.3 gather_fusion.1
  91.2 0.0 copy-start.12
  91.2 0.0 copy-start.14
  91.2 1.9 multiply_reduce_fusion.1
  93.2 0.0 copy-start.11
  93.2 0.1 multiply_convert_fusion
  93.3 0.2 convolution_convert_fusion.1
  93.5 0.0 copy-done.6
  93.5 0.2 convolution_convert_fusion.2
  93.7 0.2 convolution_convert_fusion.3
  93.9 56.4 %all_gather.22 = bf16[2048,128]{1,0:T(8,128)(2,1)S(1)} all-gather(bf16[64,128]{1,0:T(8,128)(2,1)S(1)} %convolution_convert_fusion.2), channel_id=1, replica_groups=mesh['seq'=32,'head'=8,'doc'=2] {'seq'}, dimensions={0}, use_global_device_ids=true | all-gather | bytes 540672 | tf_op jit(solution)/shard_map/all_gather | solution.py:75
  150.2 0.8 copy-done.2
  151.0 0.0 copy-done.12
  151.0 0.4 fusion.55
  151.5 48.4 %all_gather.23 = bf16[2048,128]{1,0:T(8,128)(2,1)S(1)} all-gather(bf16[64,128]{1,0:T(8,128)(2,1)S(1)} %convolution_convert_fusion.1), channel_id=1, replica_groups=mesh['seq'=32,'head'=8,'doc'=2] {'seq'}, dimensions={0}, use_global_device_ids=true | all-gather | bytes 540672 | tf_op jit(solution)/shard_map/all_gather | solution.py:76
  199.9 0.2 fusion.26
  200.1 0.5 copy-done.3
  200.7 1.0 multiply_reduce_fusion.2
  201.7 0.9 stack.2
  202.6 6.7 %all-to-all-start = ((bf16[32,64,128]{2,1,0:T(8,128)(2,1)}), bf16[32,64,128]{2,1,0:T(8,128)(2,1)S(1)}, u32[]{:S(2)}, u32[]{:S(2)}) async-start(bf16[32,64,128]{2,1,0:T(8,128)(2,1)} %stack.2), calls=%async_computation | async-start | bytes 1048576 | tf_op jit(solution)/shard_map/all_to_all | solution.py:38
  209.3 0.0 all-reduce.6.cloned.1.call-start
  209.3 0.3 dynamic-update-slice.2
  209.6 0.1 fusion.53
  209.7 127.6 %all-reduce.3 = (f32[2048]{0:T(1024)S(1)}, f32[2048]{0:T(1024)S(1)}) all-reduce(f32[2048]{0:T(1024)S(1)} %get-tuple-element.5, f32[2048]{0:T(1024)S(1)} %dynamic-update-slice.2), channel_id=2, replica_groups=mesh['seq'=32,'head'=8,'doc'=2] {'seq'}, use_global_device_ids=true, to_apply=%add.1 | all-reduce | flops 4096 | bytes 32768
  337.4 66.1 %all_gather.24 = bf16[2048,128]{1,0:T(8,128)(2,1)} all-gather(bf16[64,128]{1,0:T(8,128)(2,1)S(1)} %convolution_convert_fusion.3), channel_id=1, replica_groups=mesh['seq'=32,'head'=8,'doc'=2] {'seq'}, dimensions={0}, use_global_device_ids=true | all-gather | bytes 540672 | tf_op jit(solution)/shard_map/all_gather | solution.py:117
  403.4 1.7 fusion.19
  405.1 1.9 fusion.56
  407.0 2.2 fusion.5
  409.2 0.0 all-to-all-done
  409.2 1.5 fusion.18
  410.7 1.2 convolution_add_fusion.1
  411.9 2.1 fusion.13
  414.1 0.0 all-reduce.6.cloned.1.call-update
  414.1 77.8 %all-reduce.6.cloned.1.call-done = bf16[64,1024]{1,0:T(8,128)(2,1)} async-done(((bf16[64,1024]{1,0:T(8,128)(2,1)}), bf16[64,1024]{1,0:T(8,128)(2,1)}) %all-reduce.6.cloned.1.call-update) | async-done | bytes 131088 | tf_op jit(solution)/shard_map/psum | solution.py:185
  491.9 1.0 multiply_reduce_fusion
  493.0 1.7 fusion.39
  494.7 2.7 scatter_custom_fusion
  497.3 0.8 slice.50
  498.1 3.5 collective-permute-start.1
  501.6 1.8 constant_dynamic-update-slice_fusion.1
  503.4 2.6 collective-permute-done.1
  506.0 2.2 fusion.8
  508.2 0.0 copy-done.5
  508.2 4.2 scatter_custom_fusion.1
  512.5 2.7 convert_element_type.113
  (35 shorter events, 0.1 us)
Async XLA Ops:
  7.2 84.0 %copy-start = (bf16[1024,1024]{1,0:T(8,128)(2,1)S(1)}, bf16[1024,1024]{1,0:T(8,128)(2,1)}, u32[]{:S(2)}) copy-start(bf16[1024,1024]{1,0:T(8,128)(2,1)} %param.14) | copy-start | bytes 6291460
  8.1 76.2 %collective-permute-start = (bf16[3,1024]{1,0:T(4,128)(2,1)S(1)}, bf16[3,1024]{1,0:T(4,128)(2,1)S(1)}, u32[]{:S(2)}, u32[]{:S(2)}) collective-permute-start(bf16[3,1024]{1,0:T(4,128)(2,1)S(1)} %slice.68), channel_id=1, source_target_pairs={{0,16},{16,32},{32,48},{48,64},{64,80},{80,96},{96,112},{112,128},... | collective-permute-start | bytes 18440 | tf_op jit(solution)/shard_map/ppermute | solution.py:16
  11.3 70.2 %copy-start.16 = (s32[64]{0:T(128)}, s32[64]{0:T(128)S(1)}, u32[]{:S(2)}) copy-start(s32[64]{0:T(128)S(1)} %get-tuple-element.29) | copy-start | bytes 772
  89.8 3.3 copy-start.9
  91.2 2.1 copy-start.8
  91.2 2.3 copy-start.6
  91.2 2.5 copy-start.7
  91.2 59.8 %copy-start.12 = (pred[2048]{0:T(1024)(128)(4,1)S(1)}, pred[2048]{0:T(1024)(128)(4,1)}, u32[]{:S(2)}) copy-start(pred[2048]{0:T(1024)(128)(4,1)} %broadcast_compare_fusion) | copy-start | bytes 6148
  91.2 59.8 %copy-start.14 = (s32[64]{0:T(128)S(1)}, s32[64]{0:T(128)}, u32[]{:S(2)}) copy-start(s32[64]{0:T(128)} %iota_add_fusion) | copy-start | bytes 772
  93.2 107.5 %copy-start.11 = (bf16[64,128]{1,0:T(8,128)(2,1)S(1)}, bf16[64,128]{1,0:T(8,128)(2,1)}, u32[]{:S(2)}) copy-start(bf16[64,128]{1,0:T(8,128)(2,1)} %param.21) | copy-start | bytes 49156
  93.2 107.5 %copy-start.13 = (pred[64]{0:T(512)(128)(4,1)S(1)}, pred[64]{0:T(512)(128)(4,1)}, u32[]{:S(2)}) copy-start(pred[64]{0:T(512)(128)(4,1)} %iota_compare_fusion.2) | copy-start | bytes 196
  150.2 0.8 copy-start.2
  199.9 0.8 copy-start.3
  201.7 205.3 %copy-start.15 = (s32[64]{0:T(128)S(1)}, s32[64]{0:T(128)}, u32[]{:S(2)}) copy-start(s32[64]{0:T(128)} %iota_add_fusion) | copy-start | bytes 772
  202.6 206.6 %all-to-all-start = ((bf16[32,64,128]{2,1,0:T(8,128)(2,1)}), bf16[32,64,128]{2,1,0:T(8,128)(2,1)S(1)}, u32[]{:S(2)}, u32[]{:S(2)}) async-start(bf16[32,64,128]{2,1,0:T(8,128)(2,1)} %stack.2), calls=%async_computation | async-start | bytes 1048576 | tf_op jit(solution)/shard_map/all_to_all | solution.py:38
  209.3 282.7 %all-reduce.6.cloned.1.call-start = ((), (), s32[]{:S(2)}) async-start(), calls=%async_computation.1 | async-start | bytes 262144 | tf_op jit(solution)/shard_map/psum | solution.py:185
  405.1 4.1 copy-start.4
  498.1 7.9 %copy-start.1 = (f32[512,1024]{1,0:T(8,128)S(1)}, f32[512,1024]{1,0:T(8,128)}, u32[]{:S(2)}) copy-start(f32[512,1024]{1,0:T(8,128)} %scatter_custom_fusion) | copy-start | bytes 6291460
  498.1 7.9 %copy-start.10 = (f32[1,1024]{1,0:T(1,128)S(1)}, f32[1,1024]{1,0:T(1,128)}, u32[]{:S(2)}) copy-start(f32[1,1024]{1,0:T(1,128)} %get-tuple-element.18) | copy-start | bytes 12292
  498.1 7.9 %collective-permute-start.1 = (f32[3,1024]{1,0:T(4,128)S(1)}, f32[3,1024]{1,0:T(4,128)S(1)}, u32[]{:S(2)}, u32[]{:S(2)}) collective-permute-start(f32[3,1024]{1,0:T(4,128)S(1)} %slice.50), channel_id=1, source_target_pairs={{16,0},{32,16},{48,32},{64,48},{80,64},{96,80},{112,96},{128,112},... | collective-permute-start | bytes 36872 | tf_op jit(solution)/shard_map/ppermute | solution.py:16
  506.0 2.2 copy-start.5
Sparse Core Ops, SparseCore 0:
  414.2 77.6 all-reduce.5
